TPU v7x, 512 devices: a whole 4x4x16 slice. The times are simulated.
512 devices in a mesh: ctx: 64 (over z, y_hi, core), head: 8 (over y_lo, x).
Axes of the slice: x: 4, y: 4 (y_hi: 2, y_lo: 2; y = y_hi * 2 + y_lo), z: 16, core: 2. Of those that a mesh axis runs over, the one named last changes fastest.
Arguments:
- query_states: bfloat16 [32768, 8192], P('ctx', 'head'), may hold values from -5 to 5
- key_states: bfloat16 [32768, 1024], P('ctx', 'head'), may hold values from -5 to 5
- value_states: bfloat16 [32768, 1024], P('ctx', 'head'), may hold values from -6 to 6
- out_grad: bfloat16 [32768, 8192], P('ctx', 'head'), may hold values from -6 to 6
- block_lists: int32 [256, 4], replicated, may hold values from 0 to 255, as said below
Outputs:
- query_grad: bfloat16 [32768, 8192], P(('ctx', 'head'))
- key_grad: bfloat16 [32768, 1024], P(('ctx', 'head'))
- value_grad: bfloat16 [32768, 1024], P(('ctx', 'head'))
Inputs may be any that keep to these rules, and one draw needn't show every extreme that they name: `block_lists`: entry 0 of row b is b. The other entries name distinct blocks below b, each held by the same index of ctx as b or by one of the 8 indices just below it; a row with fewer candidates repeats b in its remaining entries. Taken over the 4 rows of one index of ctx, the listed blocks that another index of ctx holds are at most one distinct block.
All inputs are finite; a program needn't handle non-finite values.
Results may differ from a plain program's by a relative error of at most 0.012.
Values may be sent and summed in bfloat16 or wider, within the bound.
No kernel may reach another device: no remote copies, remote signals or barrier semaphores. Data moves between devices by JAX's collectives and lax.ppermute only.
A program may use at most 64 MiB of HBM per device.

v0:
```python
import math
import jax
import jax.numpy as jnp
from jax import lax
from jax.sharding import PartitionSpec as P

HEADS = 64
KV_HEADS = 8
HEAD_DIM = 128
BLOCK = 128
REACH = 8


def from_behind(x, axis, by):
    devices = lax.axis_size(axis)
    pairs = [(i, i + by) for i in range(devices) if 0 <= i + by < devices]
    return lax.ppermute(x, axis, pairs)


def block_grads(query_blk, grad_blk, kv_blk, entries, block_ids):
    kv_cols = kv_blk.shape[-1] // 2
    kv_heads = kv_cols // HEAD_DIM
    leading = kv_blk.shape[:3]
    scaling = 1.0 / math.sqrt(HEAD_DIM)
    key_blk = kv_blk[..., :kv_cols].reshape(leading + (kv_heads, HEAD_DIM))
    value_blk = kv_blk[..., kv_cols:].reshape(leading + (kv_heads, HEAD_DIM))
    chosen = entries.shape[1]
    order_ids = jnp.arange(chosen, dtype=jnp.int32)
    repeat = (entries[:, :, None] == entries[:, None, :]) & (
        order_ids[None, None, :] < order_ids[None, :, None]
    )
    usable = jnp.logical_not(jnp.any(repeat, axis=2))
    positions = jnp.arange(BLOCK, dtype=jnp.int32)
    causal = positions[None, :] <= positions[:, None]
    earlier = entries < block_ids[:, None]
    allowed = usable[:, None, :, None] & (earlier[:, None, :, None] | causal[None, :, None, :])
    allowed = allowed[:, None, None]
    scores = (
        jnp.einsum("nighd,netgd->nghiet", query_blk, key_blk, preferred_element_type=jnp.float32)
        * scaling
    )
    scores = jnp.where(allowed, scores, -1e30)
    row_max = jnp.max(scores, axis=(4, 5), keepdims=True)
    total = jnp.sum(jnp.where(allowed, jnp.exp(scores - row_max), 0.0), axis=(4, 5), keepdims=True)
    log_total = row_max + jnp.log(total)
    prob = jnp.where(allowed, jnp.exp(scores - log_total), 0.0)
    prob_half = prob.astype(jnp.bfloat16)
    output = jnp.einsum(
        "nghiet,netgd->nighd", prob_half, value_blk, preferred_element_type=jnp.float32
    ).astype(jnp.bfloat16)
    output_wide = lax.optimization_barrier(output).astype(jnp.float32)
    row_dot = jnp.sum(grad_blk.astype(jnp.float32) * output_wide, axis=-1)
    prob_grad = jnp.einsum(
        "nighd,netgd->nghiet", grad_blk, value_blk, preferred_element_type=jnp.float32
    )
    centred = prob_grad - jnp.transpose(row_dot, (0, 2, 3, 1))[..., None, None]
    score_grad = (prob * centred * scaling).astype(jnp.bfloat16)
    block_qgrad = jnp.einsum(
        "nghiet,netgd->nighd", score_grad, key_blk, preferred_element_type=jnp.float32
    ).astype(jnp.bfloat16)
    key_part = jnp.einsum(
        "nghiet,nighd->netgd", score_grad, query_blk, preferred_element_type=jnp.float32
    )
    value_part = jnp.einsum(
        "nghiet,nighd->netgd", prob_half, grad_blk, preferred_element_type=jnp.float32
    )
    pair_terms = jnp.concatenate(
        [key_part.reshape(leading + (kv_cols,)), value_part.reshape(leading + (kv_cols,))], axis=-1
    )
    return (block_qgrad, pair_terms)


def fetch_block(outgoing_one, distance):
    return from_behind(outgoing_one, "ctx", distance)


def return_block(terms_one, distance):
    return from_behind(terms_one.astype(jnp.bfloat16), "ctx", -distance).astype(terms_one.dtype)


def body(query_states, key_states, value_states, out_grad, block_lists):
    ctx_count = lax.axis_size("ctx")
    myself = lax.axis_index("ctx")
    tok_rows = query_states.shape[0]
    kv_cols = key_states.shape[1]
    kv_heads = kv_cols // HEAD_DIM
    group_size = HEADS // KV_HEADS
    blocks_here = tok_rows // BLOCK
    chosen = block_lists.shape[1]
    lists_by_dev = block_lists.reshape(ctx_count, blocks_here * chosen)
    slot_ids = jnp.arange(blocks_here, dtype=jnp.int32)
    distances = jnp.arange(1, REACH + 1, dtype=jnp.int32)
    targets = myself + distances
    target_ok = targets < ctx_count
    target_rows = jnp.take(lists_by_dev, jnp.minimum(targets, ctx_count - 1), axis=0)
    mine = target_rows // blocks_here == myself
    requested = jnp.max(jnp.where(mine, target_rows % blocks_here, -1), axis=1)
    requested = jnp.where(target_ok, requested, -1)
    kv_local = jnp.concatenate([key_states, value_states], axis=1).reshape(
        blocks_here, BLOCK, 2 * kv_cols
    )
    pick_rows = (requested[:, None] == slot_ids[None, :]).astype(jnp.bfloat16)
    outgoing = jnp.einsum(
        "sj,jtc->stc", pick_rows, kv_local, preferred_element_type=jnp.float32
    ).astype(jnp.bfloat16)
    arrivals = []
    for distance in range(1, REACH + 1):
        arrivals.append(fetch_block(outgoing[distance - 1], distance))
    incoming = jnp.stack(arrivals, axis=0)
    own_entries = lax.dynamic_slice_in_dim(block_lists, myself * blocks_here, blocks_here, 0)
    flat_entries = own_entries.reshape(blocks_here * chosen)
    behind = myself - flat_entries // blocks_here
    at_home = behind == 0
    source_row = jnp.where(at_home, REACH + flat_entries % blocks_here, behind - 1)
    kv_stock = jnp.concatenate([incoming, kv_local], axis=0)
    gathered = jnp.take(kv_stock, source_row, axis=0).reshape(
        blocks_here, chosen, BLOCK, 2 * kv_cols
    )
    per_step = 1
    step_count = blocks_here // per_step
    query_steps = query_states.reshape(step_count, per_step, BLOCK, kv_heads, group_size, HEAD_DIM)
    grad_steps = out_grad.reshape(step_count, per_step, BLOCK, kv_heads, group_size, HEAD_DIM)
    kv_steps = gathered.reshape(step_count, per_step, chosen, BLOCK, 2 * kv_cols)
    entry_steps = own_entries.reshape(step_count, per_step, chosen)
    block_steps = (myself * blocks_here + slot_ids).reshape(step_count, per_step)

    def one_step(pieces):
        return block_grads(pieces[0], pieces[1], pieces[2], pieces[3], pieces[4])

    qgrad_steps, pair_steps = lax.map(
        one_step, (query_steps, grad_steps, kv_steps, entry_steps, block_steps)
    )
    query_local = qgrad_steps.reshape(tok_rows, kv_heads * group_size * HEAD_DIM)
    pair_terms = pair_steps.reshape(blocks_here * chosen, BLOCK, 2 * kv_cols)
    keep_home = (
        at_home[None, :] & ((flat_entries % blocks_here)[None, :] == slot_ids[:, None])
    ).astype(jnp.float32)
    totals = jnp.einsum("jp,ptc->jtc", keep_home, pair_terms, precision=lax.Precision.HIGHEST)
    by_distance = behind[None, :] == distances[:, None]
    sendback = jnp.einsum(
        "sp,ptc->stc", by_distance.astype(jnp.float32), pair_terms, precision=lax.Precision.HIGHEST
    )
    returned = []
    for distance in range(1, REACH + 1):
        returned.append(return_block(sendback[distance - 1], distance))
    arrived = jnp.stack(returned, axis=0)
    credit = (requested[None, :] == slot_ids[:, None]).astype(jnp.float32)
    totals = totals + jnp.einsum("js,stc->jtc", credit, arrived, precision=lax.Precision.HIGHEST)
    key_local = totals[..., :kv_cols].reshape(tok_rows, kv_cols).astype(jnp.bfloat16)
    value_local = totals[..., kv_cols:].reshape(tok_rows, kv_cols).astype(jnp.bfloat16)
    query_grad, key_grad, value_grad = (
        lax.all_to_all(query_local, "head", split_axis=0, concat_axis=1, tiled=True),
        lax.all_to_all(key_local, "head", split_axis=0, concat_axis=1, tiled=True),
        lax.all_to_all(value_local, "head", split_axis=0, concat_axis=1, tiled=True),
    )
    return (query_grad, key_grad, value_grad)


def solution(mesh):
    in_specs = (P("ctx", "head"), P("ctx", "head"), P("ctx", "head"), P("ctx", "head"), P())
    out_specs = (P(("ctx", "head"), None), P(("ctx", "head"), None), P(("ctx", "head"), None))
    return jax.shard_map(body, mesh=mesh, in_specs=in_specs, out_specs=out_specs, check_vma=False)
```

profile of v0, /device:TPU:64, one launch (start us, length us, event | category | flops | bytes accessed | tf_op | source)
XLA Modules:
  0.0 164.2 jit_solution(14954413630219802681)
XLA Ops:
  0.7 0.8 copy.328
  2.4 1.0 pad_maximum_fusion
  3.8 0.9 fusion.55
  5.4 1.9 %collective-permute-start = (bf16[128,256]{1,0:T(8,128)(2,1)}, bf16[128,256]{1,0:T(8,128)(2,1)}, u32[]{:S(2)}, u32[]{:S(2)}) collective-permute-start(bf16[128,256]{1,0:T(8,128)(2,1)} %bitcast.256), channel_id=1, source_target_pairs={{0,8},{8,16},{16,24},{24,32},{32,40},{40,48},{48,56},{56,64},{64,7... | collective-permute-start | bytes 196616 | tf_op jit(solution)/shard_map/ppermute | solution.py:17
  7.9 5.1 %collective-permute-start.1 = (bf16[128,256]{1,0:T(8,128)(2,1)}, bf16[128,256]{1,0:T(8,128)(2,1)}, u32[]{:S(2)}, u32[]{:S(2)}) collective-permute-start(bf16[128,256]{1,0:T(8,128)(2,1)} %bitcast.255), channel_id=1, source_target_pairs={{0,16},{8,24},{16,32},{24,40},{32,48},{40,56},{48,64},{56,72},{64,... | collective-permute-start | bytes 196616 | tf_op jit(solution)/shard_map/ppermute | solution.py:17
  13.7 6.2 %collective-permute-start.2 = (bf16[128,256]{1,0:T(8,128)(2,1)}, bf16[128,256]{1,0:T(8,128)(2,1)}, u32[]{:S(2)}, u32[]{:S(2)}) collective-permute-start(bf16[128,256]{1,0:T(8,128)(2,1)} %bitcast.254), channel_id=1, source_target_pairs={{0,24},{8,32},{16,40},{24,48},{32,56},{40,64},{48,72},{56,80},{64,... | collective-permute-start | bytes 196616 | tf_op jit(solution)/shard_map/ppermute | solution.py:17
  19.9 5.0 %collective-permute-start.3 = (bf16[128,256]{1,0:T(8,128)(2,1)S(1)}, bf16[128,256]{1,0:T(8,128)(2,1)}, u32[]{:S(2)}, u32[]{:S(2)}) collective-permute-start(bf16[128,256]{1,0:T(8,128)(2,1)S(1)} %bitcast.319), channel_id=1, source_target_pairs={{0,32},{8,40},{16,48},{24,56},{32,64},{40,72},{48,80},{56,88},{64,... | collective-permute-start | bytes 196616 | tf_op jit(solution)/shard_map/ppermute | solution.py:17
  25.0 1.9 %collective-permute-start.4 = (bf16[128,256]{1,0:T(8,128)(2,1)S(1)}, bf16[128,256]{1,0:T(8,128)(2,1)}, u32[]{:S(2)}, u32[]{:S(2)}) collective-permute-start(bf16[128,256]{1,0:T(8,128)(2,1)S(1)} %bitcast.318), channel_id=1, source_target_pairs={{0,40},{8,48},{16,56},{24,64},{32,72},{40,80},{48,88},{56,96},{64,... | collective-permute-start | bytes 196616 | tf_op jit(solution)/shard_map/ppermute | solution.py:17
  29.0 1.3 copy.400
  30.8 4.9 %collective-permute-start.5 = (bf16[128,256]{1,0:T(8,128)(2,1)S(1)}, bf16[128,256]{1,0:T(8,128)(2,1)S(1)}, u32[]{:S(2)}, u32[]{:S(2)}) collective-permute-start(bf16[128,256]{1,0:T(8,128)(2,1)S(1)} %bitcast.330), channel_id=1, source_target_pairs={{0,48},{8,56},{16,64},{24,72},{32,80},{40,88},{48,96},{56,104},{64... | collective-permute-start | bytes 196616 | tf_op jit(solution)/shard_map/ppermute | solution.py:17
  35.8 0.8 bitcast_dynamic-update-slice_fusion.7
  36.6 9.2 %collective-permute-start.6 = (bf16[128,256]{1,0:T(8,128)(2,1)S(1)}, bf16[128,256]{1,0:T(8,128)(2,1)S(1)}, u32[]{:S(2)}, u32[]{:S(2)}) collective-permute-start(bf16[128,256]{1,0:T(8,128)(2,1)S(1)} %bitcast.324), channel_id=1, source_target_pairs={{0,56},{8,64},{16,72},{24,80},{32,88},{40,96},{48,104},{56,112},{6... | collective-permute-start | bytes 196616 | tf_op jit(solution)/shard_map/ppermute | solution.py:17
  45.8 0.8 bitcast_dynamic-update-slice_fusion.6
  46.7 3.4 %collective-permute-start.7 = (bf16[128,256]{1,0:T(8,128)(2,1)S(1)}, bf16[128,256]{1,0:T(8,128)(2,1)S(1)}, u32[]{:S(2)}, u32[]{:S(2)}) collective-permute-start(bf16[128,256]{1,0:T(8,128)(2,1)S(1)} %bitcast.321), channel_id=1, source_target_pairs={{0,64},{8,72},{16,80},{24,88},{32,96},{40,104},{48,112},{56,120},{... | collective-permute-start | bytes 196616 | tf_op jit(solution)/shard_map/ppermute | solution.py:17
  50.1 0.8 bitcast_dynamic-update-slice_fusion.5
  50.9 0.8 bitcast_dynamic-update-slice_fusion.4
  51.8 0.8 bitcast_dynamic-update-slice_fusion.3
  52.7 1.2 collective-permute-done.7
  54.7 32.7 %while.12 = (s32[]{:T(128)}, bf16[4,1,128,1,8,128]{5,4,2,0,3,1:T(8,128)(2,1)}, f32[4,1,4,128,256]{3,4,2,1,0:T(8,128)}, bf16[4,1,4,128,256]{4,3,2,1,0:T(8,128)(2,...) while((s32[]{:T(128)}, ...), condition=%wide.region_6.7_spmd, body=%wide.region_1.6_spmd.sunk | while | flops 815806528 | bytes 21442768 | solution.py:130
  55.3 0.7 broadcast_compare_fusion.3
  56.3 1.0 constant_dynamic-slice_fusion.8
  59.5 0.7 fusion.85
  61.3 0.7 constant_dynamic-update-slice_fusion.3
  62.0 0.9 fusion.87
  64.5 1.0 constant_dynamic-slice_fusion.8
  67.7 0.7 fusion.85
  69.5 0.7 constant_dynamic-update-slice_fusion.3
  70.2 0.8 fusion.87
  72.7 1.0 constant_dynamic-slice_fusion.8
  75.9 0.7 fusion.85
  77.7 0.7 constant_dynamic-update-slice_fusion.3
  78.4 0.8 fusion.87
  80.8 1.0 constant_dynamic-slice_fusion.8
  84.1 0.7 fusion.85
  85.8 0.7 constant_dynamic-update-slice_fusion.3
  86.6 0.8 fusion.87
  87.4 2.2 %copy.339 = f32[16,128,256]{2,0,1:T(8,128)S(1)} copy(f32[16,128,256]{1,2,0:T(8,128)} %bitcast.313) | data formatting | bytes 4194304 | tf_op jit(solution)/shard_map/reshape | solution.py:134
  89.7 0.8 convolution_convert_fusion.1
  90.5 0.9 fusion.54
  91.5 1.9 %collective-permute-start.8 = (bf16[128,256]{1,0:T(8,128)(2,1)S(1)}, bf16[128,256]{1,0:T(8,128)(2,1)S(1)}, u32[]{:S(2)}, u32[]{:S(2)}) collective-permute-start(bf16[128,256]{1,0:T(8,128)(2,1)S(1)} %bitcast.338), channel_id=1, source_target_pairs={{8,0},{16,8},{24,16},{32,24},{40,32},{48,40},{56,48},{64,56},{72,6... | collective-permute-start | bytes 196616 | tf_op jit(solution)/shard_map/ppermute | solution.py:17
  93.4 4.4 %collective-permute-start.9 = (bf16[128,256]{1,0:T(8,128)(2,1)S(1)}, bf16[128,256]{1,0:T(8,128)(2,1)S(1)}, u32[]{:S(2)}, u32[]{:S(2)}) collective-permute-start(bf16[128,256]{1,0:T(8,128)(2,1)S(1)} %bitcast.332), channel_id=1, source_target_pairs={{16,0},{24,8},{32,16},{40,24},{48,32},{56,40},{64,48},{72,56},{80,... | collective-permute-start | bytes 196616 | tf_op jit(solution)/shard_map/ppermute | solution.py:17
  97.8 2.7 %collective-permute-start.10 = (bf16[128,256]{1,0:T(8,128)(2,1)S(1)}, bf16[128,256]{1,0:T(8,128)(2,1)S(1)}, u32[]{:S(2)}, u32[]{:S(2)}) collective-permute-start(bf16[128,256]{1,0:T(8,128)(2,1)S(1)} %bitcast.328), channel_id=1, source_target_pairs={{24,0},{32,8},{40,16},{48,24},{56,32},{64,40},{72,48},{80,56},{88,... | collective-permute-start | bytes 196616 | tf_op jit(solution)/shard_map/ppermute | solution.py:17
  100.7 2.1 %collective-permute-start.11 = (bf16[128,256]{1,0:T(8,128)(2,1)S(1)}, bf16[128,256]{1,0:T(8,128)(2,1)S(1)}, u32[]{:S(2)}, u32[]{:S(2)}) collective-permute-start(bf16[128,256]{1,0:T(8,128)(2,1)S(1)} %bitcast.333), channel_id=1, source_target_pairs={{32,0},{40,8},{48,16},{56,24},{64,32},{72,40},{80,48},{88,56},{96,... | collective-permute-start | bytes 196616 | tf_op jit(solution)/shard_map/ppermute | solution.py:17
  102.8 1.9 %collective-permute-start.12 = (bf16[128,256]{1,0:T(8,128)(2,1)S(1)}, bf16[128,256]{1,0:T(8,128)(2,1)S(1)}, u32[]{:S(2)}, u32[]{:S(2)}) collective-permute-start(bf16[128,256]{1,0:T(8,128)(2,1)S(1)} %bitcast.329), channel_id=1, source_target_pairs={{40,0},{48,8},{56,16},{64,24},{72,32},{80,40},{88,48},{96,56},{104... | collective-permute-start | bytes 196616 | tf_op jit(solution)/shard_map/ppermute | solution.py:17
  104.7 1.9 %collective-permute-start.13 = (bf16[128,256]{1,0:T(8,128)(2,1)S(1)}, bf16[128,256]{1,0:T(8,128)(2,1)S(1)}, u32[]{:S(2)}, u32[]{:S(2)}) collective-permute-start(bf16[128,256]{1,0:T(8,128)(2,1)S(1)} %bitcast.323), channel_id=1, source_target_pairs={{48,0},{56,8},{64,16},{72,24},{80,32},{88,40},{96,48},{104,56},{11... | collective-permute-start | bytes 196616 | tf_op jit(solution)/shard_map/ppermute | solution.py:17
  106.7 1.9 %collective-permute-start.14 = (bf16[128,256]{1,0:T(8,128)(2,1)S(1)}, bf16[128,256]{1,0:T(8,128)(2,1)S(1)}, u32[]{:S(2)}, u32[]{:S(2)}) collective-permute-start(bf16[128,256]{1,0:T(8,128)(2,1)S(1)} %bitcast.322), channel_id=1, source_target_pairs={{56,0},{64,8},{72,16},{80,24},{88,32},{96,40},{104,48},{112,56},{1... | collective-permute-start | bytes 196616 | tf_op jit(solution)/shard_map/ppermute | solution.py:17
  108.6 2.1 %collective-permute-start.15 = (bf16[128,256]{1,0:T(8,128)(2,1)S(1)}, bf16[128,256]{1,0:T(8,128)(2,1)S(1)}, u32[]{:S(2)}, u32[]{:S(2)}) collective-permute-start(bf16[128,256]{1,0:T(8,128)(2,1)S(1)} %bitcast.320), channel_id=1, source_target_pairs={{64,0},{72,8},{80,16},{88,24},{96,32},{104,40},{112,48},{120,56},{... | collective-permute-start | bytes 196616 | tf_op jit(solution)/shard_map/ppermute | solution.py:17
  110.7 0.8 fusion.39
  112.1 1.1 collective-permute-done.13
  113.4 1.4 collective-permute-done.14
  114.9 7.6 %collective-permute-done.15 = bf16[128,256]{1,0:T(8,128)(2,1)S(1)} collective-permute-done((bf16[128,256]{1,0:T(8,128)(2,1)S(1)}, bf16[128,256]{1,0:T(8,128)(2,1)S(1)}, u32[]{:S(2)}, u32[]{:S(2)}) %collective-permute-start.15) | collective-permute-done | bytes 65568 | tf_op jit(solution)/shard_map/ppermute | solution.py:17
  122.6 1.6 stack.78
  124.6 0.7 copy.351
  125.3 4.4 %all-to-all-start.2 = ((bf16[8,64,128]{2,1,0:T(8,128)(2,1)}), bf16[8,64,128]{2,1,0:T(8,128)(2,1)S(1)}, u32[]{:S(2)}, u32[]{:S(2)}) async-start(bf16[8,64,128]{2,1,0:T(8,128)(2,1)} %bitcast.78), calls=%async_computation.2 | async-start | bytes 262144 | tf_op jit(solution)/shard_map/all_to_all | solution.py:154
  129.7 0.7 copy.349
  130.4 5.9 %all-to-all-done.2 = bf16[8,64,128]{2,1,0:T(8,128)(2,1)S(1)} async-done(((bf16[8,64,128]{2,1,0:T(8,128)(2,1)}), bf16[8,64,128]{2,1,0:T(8,128)(2,1)S(1)}, u32[]{:S(2)}, u32[]{:S(2)}) %all-to-all-start.2) | async-done | bytes 131104 | tf_op jit(solution)/shard_map/all_to_all | solution.py:154
  136.3 3.4 %all-to-all-start.1 = ((bf16[8,64,128]{2,1,0:T(8,128)(2,1)}), bf16[8,64,128]{2,1,0:T(8,128)(2,1)S(1)}, u32[]{:S(2)}, u32[]{:S(2)}) async-start(bf16[8,64,128]{2,1,0:T(8,128)(2,1)} %bitcast.76), calls=%async_computation.1 | async-start | bytes 262144 | tf_op jit(solution)/shard_map/all_to_all | solution.py:153
  139.7 1.3 all_to_all.38
  140.9 5.2 %all-to-all-done.1 = bf16[8,64,128]{2,1,0:T(8,128)(2,1)S(1)} async-done(((bf16[8,64,128]{2,1,0:T(8,128)(2,1)}), bf16[8,64,128]{2,1,0:T(8,128)(2,1)S(1)}, u32[]{:S(2)}, u32[]{:S(2)}) %all-to-all-start.1) | async-done | bytes 131104 | tf_op jit(solution)/shard_map/all_to_all | solution.py:153
  146.2 3.6 %all-to-all-start = ((bf16[8,64,1024]{2,1,0:T(8,128)(2,1)}), bf16[8,64,1024]{2,1,0:T(8,128)(2,1)S(1)}, u32[]{:S(2)}, u32[]{:S(2)}) async-start(bf16[8,64,1024]{2,1,0:T(8,128)(2,1)} %all_to_all.38), calls=%async_computation | async-start | bytes 2097152 | tf_op jit(solution)/shard_map/all_to_all | solution.py:152
  149.7 0.7 copy_bitcast_fusion.5
  150.4 0.7 copy_bitcast_fusion.6
  151.1 12.1 %all-to-all-done = bf16[8,64,1024]{2,1,0:T(8,128)(2,1)S(1)} async-done(((bf16[8,64,1024]{2,1,0:T(8,128)(2,1)}), bf16[8,64,1024]{2,1,0:T(8,128)(2,1)S(1)}, u32[]{:S(2)}, u32[]{:S(2)}) %all-to-all-start) | async-done | bytes 1048608 | tf_op jit(solution)/shard_map/all_to_all | solution.py:152
  163.2 1.1 copy.396
  (156 shorter events, 26.3 us)
Async XLA Ops:
  2.4 1.4 copy-start.6
  2.4 25.1 %copy-start.3 = (s32[256,4]{0,1:T(4,128)S(1)}, s32[256,4]{0,1:T(4,128)}, u32[]{:S(2)}) copy-start(s32[256,4]{0,1:T(4,128)} %param.11) | copy-start | bytes 12292
  3.4 25.3 %copy-start = (bf16[512,1024]{1,0:T(8,128)(2,1)S(1)}, bf16[512,1024]{1,0:T(8,128)(2,1)}, u32[]{:S(2)}) copy-start(bf16[512,1024]{1,0:T(8,128)(2,1)} %param.7) | copy-start | bytes 3145732
  4.7 24.2 %copy-start.1 = (bf16[512,1024]{1,0:T(8,128)(2,1)S(1)}, bf16[512,1024]{1,0:T(8,128)(2,1)}, u32[]{:S(2)}) copy-start(bf16[512,1024]{1,0:T(8,128)(2,1)} %param.10) | copy-start | bytes 3145732
  5.4 25.4 %collective-permute-start = (bf16[128,256]{1,0:T(8,128)(2,1)}, bf16[128,256]{1,0:T(8,128)(2,1)}, u32[]{:S(2)}, u32[]{:S(2)}) collective-permute-start(bf16[128,256]{1,0:T(8,128)(2,1)} %bitcast.256), channel_id=1, source_target_pairs={{0,8},{8,16},{16,24},{24,32},{32,40},{40,48},{48,56},{56,64},{64,7... | collective-permute-start | bytes 196616 | tf_op jit(solution)/shard_map/ppermute | solution.py:17
  7.9 28.7 %collective-permute-start.1 = (bf16[128,256]{1,0:T(8,128)(2,1)}, bf16[128,256]{1,0:T(8,128)(2,1)}, u32[]{:S(2)}, u32[]{:S(2)}) collective-permute-start(bf16[128,256]{1,0:T(8,128)(2,1)} %bitcast.255), channel_id=1, source_target_pairs={{0,16},{8,24},{16,32},{24,40},{32,48},{40,56},{48,64},{56,72},{64,... | collective-permute-start | bytes 196616 | tf_op jit(solution)/shard_map/ppermute | solution.py:17
  13.7 33.0 %collective-permute-start.2 = (bf16[128,256]{1,0:T(8,128)(2,1)}, bf16[128,256]{1,0:T(8,128)(2,1)}, u32[]{:S(2)}, u32[]{:S(2)}) collective-permute-start(bf16[128,256]{1,0:T(8,128)(2,1)} %bitcast.254), channel_id=1, source_target_pairs={{0,24},{8,32},{16,40},{24,48},{32,56},{40,64},{48,72},{56,80},{64,... | collective-permute-start | bytes 196616 | tf_op jit(solution)/shard_map/ppermute | solution.py:17
  19.9 31.0 %collective-permute-start.3 = (bf16[128,256]{1,0:T(8,128)(2,1)S(1)}, bf16[128,256]{1,0:T(8,128)(2,1)}, u32[]{:S(2)}, u32[]{:S(2)}) collective-permute-start(bf16[128,256]{1,0:T(8,128)(2,1)S(1)} %bitcast.319), channel_id=1, source_target_pairs={{0,32},{8,40},{16,48},{24,56},{32,64},{40,72},{48,80},{56,88},{64,... | collective-permute-start | bytes 196616 | tf_op jit(solution)/shard_map/ppermute | solution.py:17
  25.0 26.8 %collective-permute-start.4 = (bf16[128,256]{1,0:T(8,128)(2,1)S(1)}, bf16[128,256]{1,0:T(8,128)(2,1)}, u32[]{:S(2)}, u32[]{:S(2)}) collective-permute-start(bf16[128,256]{1,0:T(8,128)(2,1)S(1)} %bitcast.318), channel_id=1, source_target_pairs={{0,40},{8,48},{16,56},{24,64},{32,72},{40,80},{48,88},{56,96},{64,... | collective-permute-start | bytes 196616 | tf_op jit(solution)/shard_map/ppermute | solution.py:17
  27.7 0.8 copy-start.4
  30.2 24.3 %copy-start.9 = (pred[4,4]{1,0:T(4,128)(4,1)S(1)}, pred[4,4]{1,0:T(4,128)(4,1)}, u32[]{:S(2)}) copy-start(pred[4,4]{1,0:T(4,128)(4,1)} %copy.327) | copy-start | bytes 52
  30.8 21.8 %collective-permute-start.5 = (bf16[128,256]{1,0:T(8,128)(2,1)S(1)}, bf16[128,256]{1,0:T(8,128)(2,1)S(1)}, u32[]{:S(2)}, u32[]{:S(2)}) collective-permute-start(bf16[128,256]{1,0:T(8,128)(2,1)S(1)} %bitcast.330), channel_id=1, source_target_pairs={{0,48},{8,56},{16,64},{24,72},{32,80},{40,88},{48,96},{56,104},{64... | collective-permute-start | bytes 196616 | tf_op jit(solution)/shard_map/ppermute | solution.py:17
  36.6 16.0 %collective-permute-start.6 = (bf16[128,256]{1,0:T(8,128)(2,1)S(1)}, bf16[128,256]{1,0:T(8,128)(2,1)S(1)}, u32[]{:S(2)}, u32[]{:S(2)}) collective-permute-start(bf16[128,256]{1,0:T(8,128)(2,1)S(1)} %bitcast.324), channel_id=1, source_target_pairs={{0,56},{8,64},{16,72},{24,80},{32,88},{40,96},{48,104},{56,112},{6... | collective-permute-start | bytes 196616 | tf_op jit(solution)/shard_map/ppermute | solution.py:17
  46.7 7.1 %collective-permute-start.7 = (bf16[128,256]{1,0:T(8,128)(2,1)S(1)}, bf16[128,256]{1,0:T(8,128)(2,1)S(1)}, u32[]{:S(2)}, u32[]{:S(2)}) collective-permute-start(bf16[128,256]{1,0:T(8,128)(2,1)S(1)} %bitcast.321), channel_id=1, source_target_pairs={{0,64},{8,72},{16,80},{24,88},{32,96},{40,104},{48,112},{56,120},{... | collective-permute-start | bytes 196616 | tf_op jit(solution)/shard_map/ppermute | solution.py:17
  53.9 0.8 copy-start.10
  87.4 2.2 %copy-start.8 = (s32[8]{0:T(128)S(1)}, s32[8]{0:T(128)}, u32[]{:S(2)}) copy-start(s32[8]{0:T(128)} %iota_add_fusion.1) | copy-start | bytes 100
  89.7 10.9 %copy-start.5 = (s32[16]{0:T(128)S(1)}, s32[16]{0:T(128)}, u32[]{:S(2)}) copy-start(s32[16]{0:T(128)} %copy-done.4) | copy-start | bytes 196
  91.5 13.2 %collective-permute-start.8 = (bf16[128,256]{1,0:T(8,128)(2,1)S(1)}, bf16[128,256]{1,0:T(8,128)(2,1)S(1)}, u32[]{:S(2)}, u32[]{:S(2)}) collective-permute-start(bf16[128,256]{1,0:T(8,128)(2,1)S(1)} %bitcast.338), channel_id=1, source_target_pairs={{8,0},{16,8},{24,16},{32,24},{40,32},{48,40},{56,48},{64,56},{72,6... | collective-permute-start | bytes 196616 | tf_op jit(solution)/shard_map/ppermute | solution.py:17
  93.4 13.2 %collective-permute-start.9 = (bf16[128,256]{1,0:T(8,128)(2,1)S(1)}, bf16[128,256]{1,0:T(8,128)(2,1)S(1)}, u32[]{:S(2)}, u32[]{:S(2)}) collective-permute-start(bf16[128,256]{1,0:T(8,128)(2,1)S(1)} %bitcast.332), channel_id=1, source_target_pairs={{16,0},{24,8},{32,16},{40,24},{48,32},{56,40},{64,48},{72,56},{80,... | collective-permute-start | bytes 196616 | tf_op jit(solution)/shard_map/ppermute | solution.py:17
  97.8 10.8 %collective-permute-start.10 = (bf16[128,256]{1,0:T(8,128)(2,1)S(1)}, bf16[128,256]{1,0:T(8,128)(2,1)S(1)}, u32[]{:S(2)}, u32[]{:S(2)}) collective-permute-start(bf16[128,256]{1,0:T(8,128)(2,1)S(1)} %bitcast.328), channel_id=1, source_target_pairs={{24,0},{32,8},{40,16},{48,24},{56,32},{64,40},{72,48},{80,56},{88,... | collective-permute-start | bytes 196616 | tf_op jit(solution)/shard_map/ppermute | solution.py:17
  100.7 11.2 %collective-permute-start.11 = (bf16[128,256]{1,0:T(8,128)(2,1)S(1)}, bf16[128,256]{1,0:T(8,128)(2,1)S(1)}, u32[]{:S(2)}, u32[]{:S(2)}) collective-permute-start(bf16[128,256]{1,0:T(8,128)(2,1)S(1)} %bitcast.333), channel_id=1, source_target_pairs={{32,0},{40,8},{48,16},{56,24},{64,32},{72,40},{80,48},{88,56},{96,... | collective-permute-start | bytes 196616 | tf_op jit(solution)/shard_map/ppermute | solution.py:17
  102.8 9.2 %collective-permute-start.12 = (bf16[128,256]{1,0:T(8,128)(2,1)S(1)}, bf16[128,256]{1,0:T(8,128)(2,1)S(1)}, u32[]{:S(2)}, u32[]{:S(2)}) collective-permute-start(bf16[128,256]{1,0:T(8,128)(2,1)S(1)} %bitcast.329), channel_id=1, source_target_pairs={{40,0},{48,8},{56,16},{64,24},{72,32},{80,40},{88,48},{96,56},{104... | collective-permute-start | bytes 196616 | tf_op jit(solution)/shard_map/ppermute | solution.py:17
  104.7 8.6 %collective-permute-start.13 = (bf16[128,256]{1,0:T(8,128)(2,1)S(1)}, bf16[128,256]{1,0:T(8,128)(2,1)S(1)}, u32[]{:S(2)}, u32[]{:S(2)}) collective-permute-start(bf16[128,256]{1,0:T(8,128)(2,1)S(1)} %bitcast.323), channel_id=1, source_target_pairs={{48,0},{56,8},{64,16},{72,24},{80,32},{88,40},{96,48},{104,56},{11... | collective-permute-start | bytes 196616 | tf_op jit(solution)/shard_map/ppermute | solution.py:17
  106.7 8.1 %collective-permute-start.14 = (bf16[128,256]{1,0:T(8,128)(2,1)S(1)}, bf16[128,256]{1,0:T(8,128)(2,1)S(1)}, u32[]{:S(2)}, u32[]{:S(2)}) collective-permute-start(bf16[128,256]{1,0:T(8,128)(2,1)S(1)} %bitcast.322), channel_id=1, source_target_pairs={{56,0},{64,8},{72,16},{80,24},{88,32},{96,40},{104,48},{112,56},{1... | collective-permute-start | bytes 196616 | tf_op jit(solution)/shard_map/ppermute | solution.py:17
  108.6 13.9 %collective-permute-start.15 = (bf16[128,256]{1,0:T(8,128)(2,1)S(1)}, bf16[128,256]{1,0:T(8,128)(2,1)S(1)}, u32[]{:S(2)}, u32[]{:S(2)}) collective-permute-start(bf16[128,256]{1,0:T(8,128)(2,1)S(1)} %bitcast.320), channel_id=1, source_target_pairs={{64,0},{72,8},{80,16},{88,24},{96,32},{104,40},{112,48},{120,56},{... | collective-permute-start | bytes 196616 | tf_op jit(solution)/shard_map/ppermute | solution.py:17
  111.6 12.7 %copy-start.7 = (s32[8]{0:T(128)S(1)}, s32[8]{0:T(128)}, u32[]{:S(2)}) copy-start(s32[8]{0:T(128)} %copy-done.6) | copy-start | bytes 100
  122.6 17.0 %copy-start.2 = (bf16[4,1,128,1,8,128]{5,4,2,0,3,1:T(8,128)(2,1)S(1)}, bf16[4,1,128,1,8,128]{5,4,2,0,3,1:T(8,128)(2,1)}, u32[]{:S(2)}) copy-start(bf16[4,1,128,1,8,128]{5,4,2,0,3,1:T(8,128)(2,1)} %get-tuple-element.46) | copy-start | bytes 3145732
  125.3 11.0 %all-to-all-start.2 = ((bf16[8,64,128]{2,1,0:T(8,128)(2,1)}), bf16[8,64,128]{2,1,0:T(8,128)(2,1)S(1)}, u32[]{:S(2)}, u32[]{:S(2)}) async-start(bf16[8,64,128]{2,1,0:T(8,128)(2,1)} %bitcast.78), calls=%async_computation.2 | async-start | bytes 262144 | tf_op jit(solution)/shard_map/all_to_all | solution.py:154
  136.3 9.9 %all-to-all-start.1 = ((bf16[8,64,128]{2,1,0:T(8,128)(2,1)}), bf16[8,64,128]{2,1,0:T(8,128)(2,1)S(1)}, u32[]{:S(2)}, u32[]{:S(2)}) async-start(bf16[8,64,128]{2,1,0:T(8,128)(2,1)} %bitcast.76), calls=%async_computation.1 | async-start | bytes 262144 | tf_op jit(solution)/shard_map/all_to_all | solution.py:153
  146.2 17.0 %all-to-all-start = ((bf16[8,64,1024]{2,1,0:T(8,128)(2,1)}), bf16[8,64,1024]{2,1,0:T(8,128)(2,1)S(1)}, u32[]{:S(2)}, u32[]{:S(2)}) async-start(bf16[8,64,1024]{2,1,0:T(8,128)(2,1)} %all_to_all.38), calls=%async_computation | async-start | bytes 2097152 | tf_op jit(solution)/shard_map/all_to_all | solution.py:152
where the time goes:
time: 165 us; the launch traced here: 164 us
  starting transfers between devices  68 us (41%)
  waiting for transfers between devices  34.6 us (21%)
  local copies, waits for them, and re-layouts  33.6 us (20%)
  matrix products  14.5 us (9%)
  other arithmetic  11.8 us (7%)
    ppermute x16, starting transfers between devices, from_behind(): return lax.ppermute(x, axis, pairs)  56.7 us
    all_to_all x1, waiting for transfers between devices, body(): lax.all_to_all(query_local, 'head', split_axis=0, concat_axis=1, tiled=True)  12.1 us
    ppermute x16, waiting for transfers between devices, from_behind(): return lax.ppermute(x, axis, pairs)  11.4 us
    unnamed x49, local copies, waits for them, and re-layouts  8.68 us
    dynamic_slice x12, local copies, waits for them, and re-layouts, body(): lax.map(one_step, (query_steps, grad_steps, kv_steps, entry_steps, block_...  7.2 us
    all_to_all x1, waiting for transfers between devices, body(): lax.all_to_all(value_local, 'head', split_axis=0, concat_axis=1, tiled=True)  5.91 us
    all_to_all x1, waiting for transfers between devices, body(): lax.all_to_all(key_local, 'head', split_axis=0, concat_axis=1, tiled=True)  5.24 us
    all_to_all x1, starting transfers between devices, body(): lax.all_to_all(value_local, 'head', split_axis=0, concat_axis=1, tiled=True)  4.37 us
  transfers between devices with their start and end apart: 19, of which 7 were waited for; matrix products, arithmetic and copies ran while one was open for 8% of the time, Pallas kernels for 0%

commit v1 on v0

--- a/solution.py
+++ b/solution.py
@@ -151,7 +151,12 @@
     query_grad, key_grad, value_grad = (
         lax.all_to_all(query_local, "head", split_axis=0, concat_axis=1, tiled=True),
         lax.all_to_all(key_local, "head", split_axis=0, concat_axis=1, tiled=True),
-        lax.all_to_all(value_local, "head", split_axis=0, concat_axis=1, tiled=True),
+        jnp.concatenate(
+            lax.all_to_all(
+                jnp.stack(jnp.split(value_local, lax.axis_size("head"), axis=0)), "head", 0, 0
+            ),
+            axis=1,
+        ),
     )
     return (query_grad, key_grad, value_grad)
 

time: 165 us -> 170 us (1.030)
  local copies, waits for them, and re-layouts: 33.6 us -> 37.7 us
    unnamed x49 -> x54, local copies, waits for them, and re-layouts: 8.68 us -> 12.9 us
where the time goes in v1:
time: 170 us; the launch traced here: 169 us
  starting transfers between devices  68 us (40%)
  local copies, waits for them, and re-layouts  37.7 us (22%)
  waiting for transfers between devices  34.6 us (20%)
  matrix products  14.5 us (9%)
  other arithmetic  12.4 us (7%)
    ppermute x16, starting transfers between devices, from_behind(): return lax.ppermute(x, axis, pairs)  56.7 us
    unnamed x54, local copies, waits for them, and re-layouts  12.9 us
    all_to_all x1, waiting for transfers between devices, body(): lax.all_to_all(query_local, 'head', split_axis=0, concat_axis=1, tiled=True)  12.1 us
    ppermute x16, waiting for transfers between devices, from_behind(): return lax.ppermute(x, axis, pairs)  11.4 us
    dynamic_slice x12, local copies, waits for them, and re-layouts, body(): lax.map(one_step, (query_steps, grad_steps, kv_steps, entry_steps, block_...  7.2 us
    all_to_all x1, waiting for transfers between devices, body(): lax.all_to_all(jnp.stack(jnp.split(value_local, lax.axis_size('head'), ax...  5.91 us
    all_to_all x1, waiting for transfers between devices, body(): lax.all_to_all(key_local, 'head', split_axis=0, concat_axis=1, tiled=True)  5.24 us
    all_to_all x1, starting transfers between devices, body(): lax.all_to_all(jnp.stack(jnp.split(value_local, lax.axis_size('head'), ax...  4.4 us
  transfers between devices with their start and end apart: 19, of which 7 were waited for; matrix products, arithmetic and copies ran while one was open for 8% of the time, Pallas kernels for 0%

profile of v1, /device:TPU:64, one launch (start us, length us, event | category | flops | bytes accessed | tf_op | source)
XLA Modules:
  0.0 168.9 jit_solution(11867885658273465143)
XLA Ops:
  0.7 0.8 copy.335
  2.4 1.0 pad_maximum_fusion
  3.8 0.9 fusion.55
  5.3 1.9 %collective-permute-start = (bf16[128,256]{1,0:T(8,128)(2,1)}, bf16[128,256]{1,0:T(8,128)(2,1)}, u32[]{:S(2)}, u32[]{:S(2)}) collective-permute-start(bf16[128,256]{1,0:T(8,128)(2,1)} %bitcast.288), channel_id=1, source_target_pairs={{0,8},{8,16},{16,24},{24,32},{32,40},{40,48},{48,56},{56,64},{64,7... | collective-permute-start | bytes 196616 | tf_op jit(solution)/shard_map/ppermute | solution.py:17
  7.9 5.1 %collective-permute-start.1 = (bf16[128,256]{1,0:T(8,128)(2,1)}, bf16[128,256]{1,0:T(8,128)(2,1)}, u32[]{:S(2)}, u32[]{:S(2)}) collective-permute-start(bf16[128,256]{1,0:T(8,128)(2,1)} %bitcast.287), channel_id=1, source_target_pairs={{0,16},{8,24},{16,32},{24,40},{32,48},{40,56},{48,64},{56,72},{64,... | collective-permute-start | bytes 196616 | tf_op jit(solution)/shard_map/ppermute | solution.py:17
  13.6 6.2 %collective-permute-start.2 = (bf16[128,256]{1,0:T(8,128)(2,1)}, bf16[128,256]{1,0:T(8,128)(2,1)}, u32[]{:S(2)}, u32[]{:S(2)}) collective-permute-start(bf16[128,256]{1,0:T(8,128)(2,1)} %bitcast.286), channel_id=1, source_target_pairs={{0,24},{8,32},{16,40},{24,48},{32,56},{40,64},{48,72},{56,80},{64,... | collective-permute-start | bytes 196616 | tf_op jit(solution)/shard_map/ppermute | solution.py:17
  19.8 5.0 %collective-permute-start.3 = (bf16[128,256]{1,0:T(8,128)(2,1)S(1)}, bf16[128,256]{1,0:T(8,128)(2,1)}, u32[]{:S(2)}, u32[]{:S(2)}) collective-permute-start(bf16[128,256]{1,0:T(8,128)(2,1)S(1)} %bitcast.359), channel_id=1, source_target_pairs={{0,32},{8,40},{16,48},{24,56},{32,64},{40,72},{48,80},{56,88},{64,... | collective-permute-start | bytes 196616 | tf_op jit(solution)/shard_map/ppermute | solution.py:17
  24.9 1.9 %collective-permute-start.4 = (bf16[128,256]{1,0:T(8,128)(2,1)S(1)}, bf16[128,256]{1,0:T(8,128)(2,1)}, u32[]{:S(2)}, u32[]{:S(2)}) collective-permute-start(bf16[128,256]{1,0:T(8,128)(2,1)S(1)} %bitcast.358), channel_id=1, source_target_pairs={{0,40},{8,48},{16,56},{24,64},{32,72},{40,80},{48,88},{56,96},{64,... | collective-permute-start | bytes 196616 | tf_op jit(solution)/shard_map/ppermute | solution.py:17
  27.7 0.7 copy.334
  28.9 1.3 copy.407
  30.7 4.9 %collective-permute-start.5 = (bf16[128,256]{1,0:T(8,128)(2,1)S(1)}, bf16[128,256]{1,0:T(8,128)(2,1)S(1)}, u32[]{:S(2)}, u32[]{:S(2)}) collective-permute-start(bf16[128,256]{1,0:T(8,128)(2,1)S(1)} %bitcast.370), channel_id=1, source_target_pairs={{0,48},{8,56},{16,64},{24,72},{32,80},{40,88},{48,96},{56,104},{64... | collective-permute-start | bytes 196616 | tf_op jit(solution)/shard_map/ppermute | solution.py:17
  35.7 0.8 bitcast_dynamic-update-slice_fusion.7
  36.5 9.2 %collective-permute-start.6 = (bf16[128,256]{1,0:T(8,128)(2,1)S(1)}, bf16[128,256]{1,0:T(8,128)(2,1)S(1)}, u32[]{:S(2)}, u32[]{:S(2)}) collective-permute-start(bf16[128,256]{1,0:T(8,128)(2,1)S(1)} %bitcast.364), channel_id=1, source_target_pairs={{0,56},{8,64},{16,72},{24,80},{32,88},{40,96},{48,104},{56,112},{6... | collective-permute-start | bytes 196616 | tf_op jit(solution)/shard_map/ppermute | solution.py:17
  45.8 0.8 bitcast_dynamic-update-slice_fusion.6
  46.6 3.4 %collective-permute-start.7 = (bf16[128,256]{1,0:T(8,128)(2,1)S(1)}, bf16[128,256]{1,0:T(8,128)(2,1)S(1)}, u32[]{:S(2)}, u32[]{:S(2)}) collective-permute-start(bf16[128,256]{1,0:T(8,128)(2,1)S(1)} %bitcast.361), channel_id=1, source_target_pairs={{0,64},{8,72},{16,80},{24,88},{32,96},{40,104},{48,112},{56,120},{... | collective-permute-start | bytes 196616 | tf_op jit(solution)/shard_map/ppermute | solution.py:17
  50.0 0.8 bitcast_dynamic-update-slice_fusion.5
  50.9 0.8 bitcast_dynamic-update-slice_fusion.4
  51.7 0.8 bitcast_dynamic-update-slice_fusion.3
  52.6 1.2 collective-permute-done.7
  54.4 0.8 broadcast_select_fusion
  55.3 32.7 %while.12 = (s32[]{:T(128)}, bf16[4,1,128,1,8,128]{5,4,2,0,3,1:T(8,128)(2,1)}, f32[4,1,4,128,256]{3,4,2,1,0:T(8,128)}, bf16[4,1,4,128,256]{4,3,2,1,0:T(8,128)(2,...) while((s32[]{:T(128)}, ...), condition=%wide.region_6.7_spmd, body=%wide.region_1.6_spmd.sunk | while | flops 815806528 | bytes 21442768 | solution.py:130
  56.9 1.0 constant_dynamic-slice_fusion.8
  60.1 0.7 fusion.85
  61.9 0.7 constant_dynamic-update-slice_fusion.11
  62.6 0.8 fusion.87
  65.1 1.0 constant_dynamic-slice_fusion.8
  68.3 0.7 fusion.85
  70.0 0.7 constant_dynamic-update-slice_fusion.11
  70.8 0.8 fusion.87
  73.2 1.0 constant_dynamic-slice_fusion.8
  76.4 0.7 fusion.85
  78.2 0.7 constant_dynamic-update-slice_fusion.11
  78.9 0.9 fusion.87
  81.4 1.0 constant_dynamic-slice_fusion.8
  84.6 0.7 fusion.85
  86.4 0.7 constant_dynamic-update-slice_fusion.11
  87.1 0.8 fusion.87
  88.0 2.2 %copy.346 = f32[16,128,256]{2,0,1:T(8,128)S(1)} copy(f32[16,128,256]{1,2,0:T(8,128)} %bitcast.345) | data formatting | bytes 4194304 | tf_op jit(solution)/shard_map/reshape | solution.py:134
  90.2 0.8 convolution_convert_fusion.1
  91.1 0.9 fusion.54
  92.0 1.9 %collective-permute-start.8 = (bf16[128,256]{1,0:T(8,128)(2,1)S(1)}, bf16[128,256]{1,0:T(8,128)(2,1)S(1)}, u32[]{:S(2)}, u32[]{:S(2)}) collective-permute-start(bf16[128,256]{1,0:T(8,128)(2,1)S(1)} %bitcast.378), channel_id=1, source_target_pairs={{8,0},{16,8},{24,16},{32,24},{40,32},{48,40},{56,48},{64,56},{72,6... | collective-permute-start | bytes 196616 | tf_op jit(solution)/shard_map/ppermute | solution.py:17
  93.9 4.4 %collective-permute-start.9 = (bf16[128,256]{1,0:T(8,128)(2,1)S(1)}, bf16[128,256]{1,0:T(8,128)(2,1)S(1)}, u32[]{:S(2)}, u32[]{:S(2)}) collective-permute-start(bf16[128,256]{1,0:T(8,128)(2,1)S(1)} %bitcast.372), channel_id=1, source_target_pairs={{16,0},{24,8},{32,16},{40,24},{48,32},{56,40},{64,48},{72,56},{80,... | collective-permute-start | bytes 196616 | tf_op jit(solution)/shard_map/ppermute | solution.py:17
  98.3 2.7 %collective-permute-start.10 = (bf16[128,256]{1,0:T(8,128)(2,1)S(1)}, bf16[128,256]{1,0:T(8,128)(2,1)S(1)}, u32[]{:S(2)}, u32[]{:S(2)}) collective-permute-start(bf16[128,256]{1,0:T(8,128)(2,1)S(1)} %bitcast.368), channel_id=1, source_target_pairs={{24,0},{32,8},{40,16},{48,24},{56,32},{64,40},{72,48},{80,56},{88,... | collective-permute-start | bytes 196616 | tf_op jit(solution)/shard_map/ppermute | solution.py:17
  101.2 2.1 %collective-permute-start.11 = (bf16[128,256]{1,0:T(8,128)(2,1)S(1)}, bf16[128,256]{1,0:T(8,128)(2,1)S(1)}, u32[]{:S(2)}, u32[]{:S(2)}) collective-permute-start(bf16[128,256]{1,0:T(8,128)(2,1)S(1)} %bitcast.373), channel_id=1, source_target_pairs={{32,0},{40,8},{48,16},{56,24},{64,32},{72,40},{80,48},{88,56},{96,... | collective-permute-start | bytes 196616 | tf_op jit(solution)/shard_map/ppermute | solution.py:17
  103.3 1.9 %collective-permute-start.12 = (bf16[128,256]{1,0:T(8,128)(2,1)S(1)}, bf16[128,256]{1,0:T(8,128)(2,1)S(1)}, u32[]{:S(2)}, u32[]{:S(2)}) collective-permute-start(bf16[128,256]{1,0:T(8,128)(2,1)S(1)} %bitcast.369), channel_id=1, source_target_pairs={{40,0},{48,8},{56,16},{64,24},{72,32},{80,40},{88,48},{96,56},{104... | collective-permute-start | bytes 196616 | tf_op jit(solution)/shard_map/ppermute | solution.py:17
  105.2 1.9 %collective-permute-start.13 = (bf16[128,256]{1,0:T(8,128)(2,1)S(1)}, bf16[128,256]{1,0:T(8,128)(2,1)S(1)}, u32[]{:S(2)}, u32[]{:S(2)}) collective-permute-start(bf16[128,256]{1,0:T(8,128)(2,1)S(1)} %bitcast.363), channel_id=1, source_target_pairs={{48,0},{56,8},{64,16},{72,24},{80,32},{88,40},{96,48},{104,56},{11... | collective-permute-start | bytes 196616 | tf_op jit(solution)/shard_map/ppermute | solution.py:17
  107.1 1.9 %collective-permute-start.14 = (bf16[128,256]{1,0:T(8,128)(2,1)S(1)}, bf16[128,256]{1,0:T(8,128)(2,1)S(1)}, u32[]{:S(2)}, u32[]{:S(2)}) collective-permute-start(bf16[128,256]{1,0:T(8,128)(2,1)S(1)} %bitcast.362), channel_id=1, source_target_pairs={{56,0},{64,8},{72,16},{80,24},{88,32},{96,40},{104,48},{112,56},{1... | collective-permute-start | bytes 196616 | tf_op jit(solution)/shard_map/ppermute | solution.py:17
  109.1 2.1 %collective-permute-start.15 = (bf16[128,256]{1,0:T(8,128)(2,1)S(1)}, bf16[128,256]{1,0:T(8,128)(2,1)S(1)}, u32[]{:S(2)}, u32[]{:S(2)}) collective-permute-start(bf16[128,256]{1,0:T(8,128)(2,1)S(1)} %bitcast.360), channel_id=1, source_target_pairs={{64,0},{72,8},{80,16},{88,24},{96,32},{104,40},{112,48},{120,56},{... | collective-permute-start | bytes 196616 | tf_op jit(solution)/shard_map/ppermute | solution.py:17
  111.2 0.8 fusion.39
  112.6 1.1 collective-permute-done.13
  113.9 1.4 collective-permute-done.14
  115.4 7.6 %collective-permute-done.15 = bf16[128,256]{1,0:T(8,128)(2,1)S(1)} collective-permute-done((bf16[128,256]{1,0:T(8,128)(2,1)S(1)}, bf16[128,256]{1,0:T(8,128)(2,1)S(1)}, u32[]{:S(2)}, u32[]{:S(2)}) %collective-permute-start.15) | collective-permute-done | bytes 65568 | tf_op jit(solution)/shard_map/ppermute | solution.py:17
  123.1 1.6 stack.105
  130.0 4.4 %all-to-all-start.2 = ((bf16[8,64,128]{2,1,0:T(8,128)(2,1)}), bf16[8,64,128]{2,1,0:T(8,128)(2,1)S(1)}, u32[]{:S(2)}, u32[]{:S(2)}) async-start(bf16[8,64,128]{2,1,0:T(8,128)(2,1)} %constant_dynamic-update-slice_fusion.2), calls=%async_computation.2 | async-start | bytes 262144 | tf_op jit(solution)/shard_map/all_to_all | solution.py:155
  134.4 0.7 copy.356
  135.1 5.9 %all-to-all-done.2 = bf16[8,64,128]{2,1,0:T(8,128)(2,1)S(1)} async-done(((bf16[8,64,128]{2,1,0:T(8,128)(2,1)}), bf16[8,64,128]{2,1,0:T(8,128)(2,1)S(1)}, u32[]{:S(2)}, u32[]{:S(2)}) %all-to-all-start.2) | async-done | bytes 131104 | tf_op jit(solution)/shard_map/all_to_all | solution.py:155
  141.0 3.4 %all-to-all-start.1 = ((bf16[8,64,128]{2,1,0:T(8,128)(2,1)}), bf16[8,64,128]{2,1,0:T(8,128)(2,1)S(1)}, u32[]{:S(2)}, u32[]{:S(2)}) async-start(bf16[8,64,128]{2,1,0:T(8,128)(2,1)} %bitcast.76), calls=%async_computation.1 | async-start | bytes 262144 | tf_op jit(solution)/shard_map/all_to_all | solution.py:153
  144.4 1.3 all_to_all.29
  145.7 5.2 %all-to-all-done.1 = bf16[8,64,128]{2,1,0:T(8,128)(2,1)S(1)} async-done(((bf16[8,64,128]{2,1,0:T(8,128)(2,1)}), bf16[8,64,128]{2,1,0:T(8,128)(2,1)S(1)}, u32[]{:S(2)}, u32[]{:S(2)}) %all-to-all-start.1) | async-done | bytes 131104 | tf_op jit(solution)/shard_map/all_to_all | solution.py:153
  150.9 3.6 %all-to-all-start = ((bf16[8,64,1024]{2,1,0:T(8,128)(2,1)}), bf16[8,64,1024]{2,1,0:T(8,128)(2,1)S(1)}, u32[]{:S(2)}, u32[]{:S(2)}) async-start(bf16[8,64,1024]{2,1,0:T(8,128)(2,1)} %all_to_all.29), calls=%async_computation | async-start | bytes 2097152 | tf_op jit(solution)/shard_map/all_to_all | solution.py:152
  154.5 0.7 copy_bitcast_fusion.5
  155.1 0.7 copy_bitcast_fusion.6
  155.8 12.1 %all-to-all-done = bf16[8,64,1024]{2,1,0:T(8,128)(2,1)S(1)} async-done(((bf16[8,64,1024]{2,1,0:T(8,128)(2,1)}), bf16[8,64,1024]{2,1,0:T(8,128)(2,1)S(1)}, u32[]{:S(2)}, u32[]{:S(2)}) %all-to-all-start) | async-done | bytes 1048608 | tf_op jit(solution)/shard_map/all_to_all | solution.py:152
  167.9 1.1 copy.403
  (162 shorter events, 31.0 us)
Async XLA Ops:
  2.4 1.0 copy-start.6
  2.4 25.0 %copy-start.3 = (s32[256,4]{0,1:T(4,128)S(1)}, s32[256,4]{0,1:T(4,128)}, u32[]{:S(2)}) copy-start(s32[256,4]{0,1:T(4,128)} %param.11) | copy-start | bytes 12292
  3.4 25.2 %copy-start = (bf16[512,1024]{1,0:T(8,128)(2,1)S(1)}, bf16[512,1024]{1,0:T(8,128)(2,1)}, u32[]{:S(2)}) copy-start(bf16[512,1024]{1,0:T(8,128)(2,1)} %param.7) | copy-start | bytes 3145732
  4.7 24.2 %copy-start.1 = (bf16[512,1024]{1,0:T(8,128)(2,1)S(1)}, bf16[512,1024]{1,0:T(8,128)(2,1)}, u32[]{:S(2)}) copy-start(bf16[512,1024]{1,0:T(8,128)(2,1)} %param.10) | copy-start | bytes 3145732
  5.3 25.4 %collective-permute-start = (bf16[128,256]{1,0:T(8,128)(2,1)}, bf16[128,256]{1,0:T(8,128)(2,1)}, u32[]{:S(2)}, u32[]{:S(2)}) collective-permute-start(bf16[128,256]{1,0:T(8,128)(2,1)} %bitcast.288), channel_id=1, source_target_pairs={{0,8},{8,16},{16,24},{24,32},{32,40},{40,48},{48,56},{56,64},{64,7... | collective-permute-start | bytes 196616 | tf_op jit(solution)/shard_map/ppermute | solution.py:17
  7.9 28.7 %collective-permute-start.1 = (bf16[128,256]{1,0:T(8,128)(2,1)}, bf16[128,256]{1,0:T(8,128)(2,1)}, u32[]{:S(2)}, u32[]{:S(2)}) collective-permute-start(bf16[128,256]{1,0:T(8,128)(2,1)} %bitcast.287), channel_id=1, source_target_pairs={{0,16},{8,24},{16,32},{24,40},{32,48},{40,56},{48,64},{56,72},{64,... | collective-permute-start | bytes 196616 | tf_op jit(solution)/shard_map/ppermute | solution.py:17
  13.6 33.0 %collective-permute-start.2 = (bf16[128,256]{1,0:T(8,128)(2,1)}, bf16[128,256]{1,0:T(8,128)(2,1)}, u32[]{:S(2)}, u32[]{:S(2)}) collective-permute-start(bf16[128,256]{1,0:T(8,128)(2,1)} %bitcast.286), channel_id=1, source_target_pairs={{0,24},{8,32},{16,40},{24,48},{32,56},{40,64},{48,72},{56,80},{64,... | collective-permute-start | bytes 196616 | tf_op jit(solution)/shard_map/ppermute | solution.py:17
  19.8 31.0 %collective-permute-start.3 = (bf16[128,256]{1,0:T(8,128)(2,1)S(1)}, bf16[128,256]{1,0:T(8,128)(2,1)}, u32[]{:S(2)}, u32[]{:S(2)}) collective-permute-start(bf16[128,256]{1,0:T(8,128)(2,1)S(1)} %bitcast.359), channel_id=1, source_target_pairs={{0,32},{8,40},{16,48},{24,56},{32,64},{40,72},{48,80},{56,88},{64,... | collective-permute-start | bytes 196616 | tf_op jit(solution)/shard_map/ppermute | solution.py:17
  24.9 26.8 %collective-permute-start.4 = (bf16[128,256]{1,0:T(8,128)(2,1)S(1)}, bf16[128,256]{1,0:T(8,128)(2,1)}, u32[]{:S(2)}, u32[]{:S(2)}) collective-permute-start(bf16[128,256]{1,0:T(8,128)(2,1)S(1)} %bitcast.358), channel_id=1, source_target_pairs={{0,40},{8,48},{16,56},{24,64},{32,72},{40,80},{48,88},{56,96},{64,... | collective-permute-start | bytes 196616 | tf_op jit(solution)/shard_map/ppermute | solution.py:17
  27.7 0.8 copy-start.4
  30.7 21.8 %collective-permute-start.5 = (bf16[128,256]{1,0:T(8,128)(2,1)S(1)}, bf16[128,256]{1,0:T(8,128)(2,1)S(1)}, u32[]{:S(2)}, u32[]{:S(2)}) collective-permute-start(bf16[128,256]{1,0:T(8,128)(2,1)S(1)} %bitcast.370), channel_id=1, source_target_pairs={{0,48},{8,56},{16,64},{24,72},{32,80},{40,88},{48,96},{56,104},{64... | collective-permute-start | bytes 196616 | tf_op jit(solution)/shard_map/ppermute | solution.py:17
  36.5 16.0 %collective-permute-start.6 = (bf16[128,256]{1,0:T(8,128)(2,1)S(1)}, bf16[128,256]{1,0:T(8,128)(2,1)S(1)}, u32[]{:S(2)}, u32[]{:S(2)}) collective-permute-start(bf16[128,256]{1,0:T(8,128)(2,1)S(1)} %bitcast.364), channel_id=1, source_target_pairs={{0,56},{8,64},{16,72},{24,80},{32,88},{40,96},{48,104},{56,112},{6... | collective-permute-start | bytes 196616 | tf_op jit(solution)/shard_map/ppermute | solution.py:17
  46.6 7.2 %collective-permute-start.7 = (bf16[128,256]{1,0:T(8,128)(2,1)S(1)}, bf16[128,256]{1,0:T(8,128)(2,1)S(1)}, u32[]{:S(2)}, u32[]{:S(2)}) collective-permute-start(bf16[128,256]{1,0:T(8,128)(2,1)S(1)} %bitcast.361), channel_id=1, source_target_pairs={{0,64},{8,72},{16,80},{24,88},{32,96},{40,104},{48,112},{56,120},{... | collective-permute-start | bytes 196616 | tf_op jit(solution)/shard_map/ppermute | solution.py:17
  53.8 1.5 copy-start.9
  88.0 2.2 %copy-start.8 = (s32[8]{0:T(128)S(1)}, s32[8]{0:T(128)}, u32[]{:S(2)}) copy-start(s32[8]{0:T(128)} %iota_add_fusion.1) | copy-start | bytes 100
  90.2 10.8 %copy-start.5 = (s32[16]{0:T(128)S(1)}, s32[16]{0:T(128)}, u32[]{:S(2)}) copy-start(s32[16]{0:T(128)} %copy-done.4) | copy-start | bytes 196
  92.0 13.2 %collective-permute-start.8 = (bf16[128,256]{1,0:T(8,128)(2,1)S(1)}, bf16[128,256]{1,0:T(8,128)(2,1)S(1)}, u32[]{:S(2)}, u32[]{:S(2)}) collective-permute-start(bf16[128,256]{1,0:T(8,128)(2,1)S(1)} %bitcast.378), channel_id=1, source_target_pairs={{8,0},{16,8},{24,16},{32,24},{40,32},{48,40},{56,48},{64,56},{72,6... | collective-permute-start | bytes 196616 | tf_op jit(solution)/shard_map/ppermute | solution.py:17
  93.9 13.2 %collective-permute-start.9 = (bf16[128,256]{1,0:T(8,128)(2,1)S(1)}, bf16[128,256]{1,0:T(8,128)(2,1)S(1)}, u32[]{:S(2)}, u32[]{:S(2)}) collective-permute-start(bf16[128,256]{1,0:T(8,128)(2,1)S(1)} %bitcast.372), channel_id=1, source_target_pairs={{16,0},{24,8},{32,16},{40,24},{48,32},{56,40},{64,48},{72,56},{80,... | collective-permute-start | bytes 196616 | tf_op jit(solution)/shard_map/ppermute | solution.py:17
  98.3 10.8 %collective-permute-start.10 = (bf16[128,256]{1,0:T(8,128)(2,1)S(1)}, bf16[128,256]{1,0:T(8,128)(2,1)S(1)}, u32[]{:S(2)}, u32[]{:S(2)}) collective-permute-start(bf16[128,256]{1,0:T(8,128)(2,1)S(1)} %bitcast.368), channel_id=1, source_target_pairs={{24,0},{32,8},{40,16},{48,24},{56,32},{64,40},{72,48},{80,56},{88,... | collective-permute-start | bytes 196616 | tf_op jit(solution)/shard_map/ppermute | solution.py:17
  101.2 11.2 %collective-permute-start.11 = (bf16[128,256]{1,0:T(8,128)(2,1)S(1)}, bf16[128,256]{1,0:T(8,128)(2,1)S(1)}, u32[]{:S(2)}, u32[]{:S(2)}) collective-permute-start(bf16[128,256]{1,0:T(8,128)(2,1)S(1)} %bitcast.373), channel_id=1, source_target_pairs={{32,0},{40,8},{48,16},{56,24},{64,32},{72,40},{80,48},{88,56},{96,... | collective-permute-start | bytes 196616 | tf_op jit(solution)/shard_map/ppermute | solution.py:17
  103.3 9.2 %collective-permute-start.12 = (bf16[128,256]{1,0:T(8,128)(2,1)S(1)}, bf16[128,256]{1,0:T(8,128)(2,1)S(1)}, u32[]{:S(2)}, u32[]{:S(2)}) collective-permute-start(bf16[128,256]{1,0:T(8,128)(2,1)S(1)} %bitcast.369), channel_id=1, source_target_pairs={{40,0},{48,8},{56,16},{64,24},{72,32},{80,40},{88,48},{96,56},{104... | collective-permute-start | bytes 196616 | tf_op jit(solution)/shard_map/ppermute | solution.py:17
  105.2 8.6 %collective-permute-start.13 = (bf16[128,256]{1,0:T(8,128)(2,1)S(1)}, bf16[128,256]{1,0:T(8,128)(2,1)S(1)}, u32[]{:S(2)}, u32[]{:S(2)}) collective-permute-start(bf16[128,256]{1,0:T(8,128)(2,1)S(1)} %bitcast.363), channel_id=1, source_target_pairs={{48,0},{56,8},{64,16},{72,24},{80,32},{88,40},{96,48},{104,56},{11... | collective-permute-start | bytes 196616 | tf_op jit(solution)/shard_map/ppermute | solution.py:17
  107.1 8.1 %collective-permute-start.14 = (bf16[128,256]{1,0:T(8,128)(2,1)S(1)}, bf16[128,256]{1,0:T(8,128)(2,1)S(1)}, u32[]{:S(2)}, u32[]{:S(2)}) collective-permute-start(bf16[128,256]{1,0:T(8,128)(2,1)S(1)} %bitcast.362), channel_id=1, source_target_pairs={{56,0},{64,8},{72,16},{80,24},{88,32},{96,40},{104,48},{112,56},{1... | collective-permute-start | bytes 196616 | tf_op jit(solution)/shard_map/ppermute | solution.py:17
  109.1 13.9 %collective-permute-start.15 = (bf16[128,256]{1,0:T(8,128)(2,1)S(1)}, bf16[128,256]{1,0:T(8,128)(2,1)S(1)}, u32[]{:S(2)}, u32[]{:S(2)}) collective-permute-start(bf16[128,256]{1,0:T(8,128)(2,1)S(1)} %bitcast.360), channel_id=1, source_target_pairs={{64,0},{72,8},{80,16},{88,24},{96,32},{104,40},{112,48},{120,56},{... | collective-permute-start | bytes 196616 | tf_op jit(solution)/shard_map/ppermute | solution.py:17
  112.0 12.7 %copy-start.7 = (s32[8]{0:T(128)S(1)}, s32[8]{0:T(128)}, u32[]{:S(2)}) copy-start(s32[8]{0:T(128)} %copy-done.6) | copy-start | bytes 100
  123.1 21.3 %copy-start.2 = (bf16[4,1,128,1,8,128]{5,4,2,0,3,1:T(8,128)(2,1)S(1)}, bf16[4,1,128,1,8,128]{5,4,2,0,3,1:T(8,128)(2,1)}, u32[]{:S(2)}) copy-start(bf16[4,1,128,1,8,128]{5,4,2,0,3,1:T(8,128)(2,1)} %get-tuple-element.46) | copy-start | bytes 3145732
  130.0 11.0 %all-to-all-start.2 = ((bf16[8,64,128]{2,1,0:T(8,128)(2,1)}), bf16[8,64,128]{2,1,0:T(8,128)(2,1)S(1)}, u32[]{:S(2)}, u32[]{:S(2)}) async-start(bf16[8,64,128]{2,1,0:T(8,128)(2,1)} %constant_dynamic-update-slice_fusion.2), calls=%async_computation.2 | async-start | bytes 262144 | tf_op jit(solution)/shard_map/all_to_all | solution.py:155
  141.0 9.9 %all-to-all-start.1 = ((bf16[8,64,128]{2,1,0:T(8,128)(2,1)}), bf16[8,64,128]{2,1,0:T(8,128)(2,1)S(1)}, u32[]{:S(2)}, u32[]{:S(2)}) async-start(bf16[8,64,128]{2,1,0:T(8,128)(2,1)} %bitcast.76), calls=%async_computation.1 | async-start | bytes 262144 | tf_op jit(solution)/shard_map/all_to_all | solution.py:153
  150.9 17.0 %all-to-all-start = ((bf16[8,64,1024]{2,1,0:T(8,128)(2,1)}), bf16[8,64,1024]{2,1,0:T(8,128)(2,1)S(1)}, u32[]{:S(2)}, u32[]{:S(2)}) async-start(bf16[8,64,1024]{2,1,0:T(8,128)(2,1)} %all_to_all.29), calls=%async_computation | async-start | bytes 2097152 | tf_op jit(solution)/shard_map/all_to_all | solution.py:152
